TPU v7x, 32 devices: a whole 2x2x4 slice. The times are simulated.
32 devices in a mesh: tile: 8 (over z, y), win: 4 (over x, core).
Axes of the slice: x: 2, y: 2, z: 4, core: 2. Of those that a mesh axis runs over, the one named last changes fastest.
Arguments:
- records: bfloat16 [16, 2048, 2048], P('win', 'tile'), may hold values from -6 to 6
- pair_first: int32 [2048], P('tile'), may hold values from 0 to 255
- pair_offset: int32 [2048], P('tile'), may hold values from 1 to 255
- owners: int32 [2048, 1], P('tile'), may hold values from 0 to 7; in each aligned block of 256 rows (0 to 255, 256 to 511, ...) at most 80 rows name the same one
Outputs:
- gathers: bfloat16 [8, 8, 80, 2048], P('tile', None, None, 'win')
Inputs may be any that keep to these rules, and one draw needn't show every extreme that they name: `owners`: among the 256 pairs of one tile no owner is named more than 80 times, and in every draw some tile names some owner exactly 80 times.
All inputs are finite; a program needn't handle non-finite values.
Results may differ from a plain program's by a relative error of at most 0.0066.
Values may be sent and summed in bfloat16 or wider, within the bound.
No kernel may reach another device: no remote copies, remote signals or barrier semaphores. Data moves between devices by JAX's collectives and lax.ppermute only.
A program may use at most 128 MiB of HBM per device.

v0:
```python
import math
import jax
import jax.numpy as jnp
from jax import lax
from jax.sharding import PartitionSpec as P

BAND = 64
power_floor = 1e-06


def phase_table(rows, col_count, length):
    split = 64 if col_count % 64 == 0 else 1
    coarse = jnp.arange(col_count // split, dtype=jnp.int32) * split
    fine = jnp.arange(split, dtype=jnp.int32)
    scale = 2.0 * math.pi / length
    coarse_angle = (rows[:, None] * coarse[None, :] % length).astype(jnp.float32) * scale
    fine_angle = (rows[:, None] * fine[None, :] % length).astype(jnp.float32) * scale
    c_hi, s_hi = (jnp.cos(coarse_angle)[:, :, None], jnp.sin(coarse_angle)[:, :, None])
    c_lo, s_lo = (jnp.cos(fine_angle)[:, None, :], jnp.sin(fine_angle)[:, None, :])
    shape = (rows.shape[0], col_count)
    cosine = (c_hi * c_lo - s_hi * s_lo).reshape(shape)
    sine = (s_hi * c_lo + c_hi * s_lo).reshape(shape)
    return (cosine, sine)


def forward_matrix(length):
    cosine, sine = phase_table(jnp.arange(length // 2, dtype=jnp.int32), length, length)
    return jnp.concatenate([cosine, -sine], axis=0).astype(jnp.bfloat16)


def inverse_matrix(length, first_lag, lag_count, seg_total):
    half_bins = length // 2
    lags = jnp.arange(lag_count, dtype=jnp.int32) + first_lag
    cosine, sine = phase_table(lags, half_bins, length)
    bin_index = jnp.arange(half_bins)[None, :]
    weights = jnp.where(bin_index == 0, 1.0, 2.0).astype(jnp.float32) * (
        1.0 / math.sqrt(half_bins * seg_total)
    )
    return jnp.concatenate([weights * cosine, -weights * sine], axis=1)


def whiten(spectra, band_width):
    half_bins = spectra.shape[-2] // 2
    real_rows = spectra[..., :half_bins, :]
    imaginary = spectra[..., half_bins:, :]
    energy = real_rows * real_rows + imaginary * imaginary
    grouped = energy.shape[:-2] + (half_bins // band_width, band_width, energy.shape[-1])
    band_power = jnp.mean(energy.reshape(grouped), axis=-2, keepdims=True)
    inverse_rms = jnp.broadcast_to(lax.rsqrt(band_power + power_floor), grouped).reshape(
        energy.shape
    )
    return (spectra * jnp.concatenate([inverse_rms, inverse_rms], axis=-2)).astype(jnp.bfloat16)


def cross_terms(first_part, second_part):
    half_bins = first_part.shape[-2] // 2
    first_real = first_part[..., :half_bins, :].astype(jnp.float32)
    first_imag = first_part[..., half_bins:, :].astype(jnp.float32)
    second_real = second_part[..., :half_bins, :].astype(jnp.float32)
    second_imag = second_part[..., half_bins:, :].astype(jnp.float32)
    real_sum = first_real * second_real + first_imag * second_imag
    imag_sum = first_imag * second_real - first_real * second_imag
    return jnp.concatenate([real_sum, imag_sum], axis=-2)


def bucket_select(owner_ids, owner_count, capacity):
    onehot = (owner_ids[:, None] == jnp.arange(owner_count, dtype=jnp.int32)[None, :]).astype(
        jnp.int32
    )
    slot_rank = jnp.sum((jnp.cumsum(onehot, axis=0, dtype=jnp.int32) - 1) * onehot, axis=1)
    slot_id = owner_ids * capacity + slot_rank
    return (
        slot_id[None, :] == jnp.arange(owner_count * capacity, dtype=jnp.int32)[:, None]
    ).astype(jnp.bfloat16)


def tile_ring(mesh):
    count = mesh.shape["tile"]
    try:
        column = mesh.devices.reshape(count, -1)[:, 0]
        spots = [tuple((int(c) for c in d.coords)) for d in column]
    except (AttributeError, TypeError):
        return list(range(count))
    near = [
        [j for j in range(count) if sum((abs(a - b) for a, b in zip(spots[i], spots[j]))) == 1]
        for i in range(count)
    ]
    path, seen, budget = ([0], {0}, [20000])

    def extend():
        budget[0] -= 1
        if budget[0] < 0:
            return False
        if len(path) == count:
            return count < 3 or 0 in near[path[-1]]
        options = [j for j in near[path[-1]] if j not in seen]
        options.sort(key=lambda j: sum((1 for k in near[j] if k not in seen)))
        for j in options:
            path.append(j)
            seen.add(j)
            if extend():
                return True
            path.pop()
            seen.discard(j)
        return False

    return path if extend() else list(range(count))


def make_per_device(ring):
    count = len(ring)
    block_of = [0] * count
    for place, device in enumerate(ring):
        block_of[device] = place
    to_prev = [(ring[r], ring[(r - 1) % count]) for r in range(count)]
    to_next = [(ring[r], ring[(r + 1) % count]) for r in range(count)]

    def per_device(records, pair_first, pair_offset, owners):
        tile_count = lax.axis_size("tile")
        win_count = lax.axis_size("win")
        length = records.shape[1] * tile_count
        seg_total = records.shape[0] * win_count
        block = records.shape[2] // tile_count
        half = block // 2
        my_block = jnp.asarray(block_of, dtype=jnp.int32)[lax.axis_index("tile")]
        shifted = jnp.roll(records, -half, axis=2).reshape(
            records.shape[0], records.shape[1], tile_count, block
        )
        outgoing = jnp.concatenate([shifted[:, :, b] for b in block_of], axis=2)
        forward = forward_matrix(length)
        spectra = jnp.einsum(
            "fn,snc->sfc",
            forward,
            lax.all_to_all(outgoing, "tile", split_axis=2, concat_axis=1, tiled=True),
            preferred_element_type=jnp.float32,
        )
        whitened = whiten(spectra, BAND)
        from_prev = lax.ppermute(whitened[:, :, half:], "tile", to_next)
        from_next = lax.ppermute(whitened[:, :, :half], "tile", to_prev)
        joined = jnp.concatenate([from_prev, whitened, from_next], axis=2)
        all_first = lax.all_gather(pair_first, "tile")
        all_offset = lax.all_gather(pair_offset, "tile")
        all_owners = lax.all_gather(owners[:, 0], "tile")
        my_first = lax.dynamic_index_in_dim(all_first, my_block, 0, keepdims=False)
        my_offset = lax.dynamic_index_in_dim(all_offset, my_block, 0, keepdims=False)
        my_owners = lax.dynamic_index_in_dim(all_owners, my_block, 0, keepdims=False)
        channel_ids = jnp.arange(joined.shape[2], dtype=jnp.int32)[:, None]
        pick_first = (channel_ids == my_first[None, :]).astype(jnp.bfloat16)
        pick_second = (channel_ids == (my_first + my_offset)[None, :]).astype(jnp.bfloat16)
        first_part = jnp.einsum(
            "sfc,cp->sfp", joined, pick_first, preferred_element_type=jnp.float32
        )
        second_part = jnp.einsum(
            "sfc,cp->sfp", joined, pick_second, preferred_element_type=jnp.float32
        )
        cross = jnp.sum(cross_terms(first_part, second_part), axis=0)
        lag_count = length // win_count
        stacked = lax.psum(cross, "win")
        inverse = inverse_matrix(length, lax.axis_index("win") * lag_count, lag_count, seg_total)
        correlation = jnp.dot(inverse, stacked, precision=lax.Precision.HIGHEST)
        capacity = 5 * pair_first.shape[0] // (2 * tile_count)
        chooser = bucket_select(my_owners, tile_count, capacity)
        picked = lax.dot_general(
            chooser,
            correlation.astype(jnp.bfloat16),
            (((1,), (1,)), ((), ())),
            preferred_element_type=jnp.float32,
        )
        buckets = picked.astype(jnp.bfloat16).reshape(tile_count, capacity, lag_count)
        received = lax.all_to_all(buckets, "tile", split_axis=0, concat_axis=0, tiled=True)
        ordered = jnp.stack([received[d] for d in ring], axis=0)
        return ordered[None]

    return per_device


def solution(mesh):
    placed = (P("win", "tile", None), P("tile"), P("tile"), P("tile", None))
    return jax.shard_map(
        make_per_device(tile_ring(mesh)),
        mesh=mesh,
        in_specs=placed,
        out_specs=P("tile", None, None, "win"),
        check_vma=False,
    )
```

profile of v0, /device:TPU:0, one launch (start us, length us, event | category | flops | bytes accessed | tf_op | source)
XLA Modules:
  0.0 392.1 jit_solution(10754620685707993327)
XLA Ops:
  6.5 4.3 %slice.87 = bf16[4,256,1920]{2,1,0:T(8,128)(2,1)} slice(bf16[4,256,2048]{2,1,0:T(8,128)(2,1)} %param.5), slice={[0:4], [0:256], [128:2048]} | slice | bytes 7864320 | tf_op jit(solution)/shard_map/jit(_roll_static)/slice | solution.py:126
  10.8 6.3 %copy.65 = bf16[4,256,1920]{1,2,0:T(8,128)(2,1)} copy(bf16[4,256,1920]{2,1,0:T(8,128)(2,1)} %slice.87) | data formatting | bytes 7864320
  17.3 2.4 pad_maximum_fusion.1
  20.0 17.2 %copy.52 = bf16[4,256,2048]{1,0,2:T(4,128)(2,1)} copy(bf16[4,256,2048]{1,2,0:T(8,128)(2,1)S(1)} %fusion.15) | data formatting | bytes 8388608 | tf_op jit(solution)/shard_map/concatenate | solution.py:129
  37.2 7.3 %all-to-all-start = ((bf16[4,256,2048]{1,0,2:T(4,128)(2,1)}), bf16[4,256,2048]{1,0,2:T(4,128)(2,1)}, u32[]{:S(2)}, u32[]{:S(2)}) async-start(bf16[4,256,2048]{1,0,2:T(4,128)(2,1)} %copy.52), calls=%async_computation | async-start | bytes 8388608 | tf_op jit(solution)/shard_map/all_to_all | solution.py:134
  46.2 5.2 %subtract_convert_fusion = (bf16[1024,32,64]{0,2,1:T(8,128)(2,1)}, bf16[1024,32,64]{0,2,1:T(8,128)(2,1)}) fusion(f32[1024,64]{0,1:T(8,128)S(1)} %get-tuple-element.21, f32[1024,32]{0,1:T(8,128)S(1)} %get-tuple-element.20, f32[1024,64]{0,1:T(8,128)S(1)} %get-tuple-element.22, f32[1024,32]{0,1:T(8,128)S(1)} %get-tuple-element.19), kind=kLoop, calls=%fused_computation.9 | loop fusion | flops 18874368 | bytes 9175040 | tf_op jit(solution)/shard_map/convert.3
  51.4 6.5 %copy.55 = bf16[1024,2048]{1,0:T(8,128)(2,1)} copy(bf16[1024,2048]{0,1:T(8,128)(2,1)} %bitcast.102) | data formatting | bytes 8388608 | tf_op jit(solution)/shard_map/sub | solution.py:21
  57.8 6.5 %copy.56 = bf16[1024,2048]{1,0:T(8,128)(2,1)} copy(bf16[1024,2048]{0,1:T(8,128)(2,1)} %bitcast.101) | data formatting | bytes 8388608 | tf_op jit(solution)/shard_map/neg | solution.py:28
  64.3 73.5 %all-to-all-done = bf16[4,256,2048]{1,0,2:T(4,128)(2,1)} async-done(((bf16[4,256,2048]{1,0,2:T(4,128)(2,1)}), bf16[4,256,2048]{1,0,2:T(4,128)(2,1)}, u32[]{:S(2)}, u32[]{:S(2)}) %all-to-all-start) | async-done | bytes 4194336 | tf_op jit(solution)/shard_map/all_to_all | solution.py:134
  137.8 2.7 copy.53
  140.5 2.7 copy.73
  144.2 11.7 %fusion.4 = f32[4,2048,256]{1,2,0:T(8,128)S(1)} fusion(bf16[4,2048,256]{1,2,0:T(8,128)(2,1)} %bitcast.105, bf16[1024,2048]{1,0:T(8,128)(2,1)} %copy.56, bf16[1024,2048]{1,0:T(8,128)(2,1)S(1)} %copy-done.3), kind=kOutput, calls=%fused_computation.10 | convolution fusion | flops 8606711808 | bytes 20971520 | tf_op jit(solution)/shard_map/fn,snc->sfc/dot_general | solution.py:131
  156.0 3.2 copy-done
  159.2 2.9 fusion.5
  162.1 5.4 %copy.57 = f32[4,1024,256]{2,1,0:T(8,128)} copy(f32[4,1024,256]{1,2,0:T(8,128)} %fusion.5) | data formatting | bytes 8388608 | tf_op jit(solution)/shard_map/add | solution.py:46
  167.5 2.7 bitcast_reduce_fusion
  170.2 2.3 broadcast_in_dim.12
  172.5 5.4 %copy.58 = f32[4,1024,256]{1,2,0:T(8,128)} copy(f32[4,1024,256]{2,1,0:T(8,128)} %bitcast.104) | data formatting | bytes 8388608 | tf_op jit(solution)/shard_map/reshape | solution.py:49
  177.9 7.0 %fusion.3 = bf16[4,2048,256]{1,2,0:T(8,128)(2,1)S(1)} fusion(f32[4,2048,256]{1,2,0:T(8,128)} %copy-done, f32[4,1024,256]{1,2,0:T(8,128)} %copy.58), kind=kLoop, calls=%fused_computation.5 | loop fusion | flops 6291456 | bytes 16777216 | tf_op jit(solution)/shard_map/convert_element_type | solution.py:52
  184.9 2.1 fusion.66
  187.5 1.5 collective-permute-start
  191.4 56.6 %all-gather = s32[2048,1]{0,1:T(1,128)S(1)} all-gather(s32[256,1]{0,1:T(1,128)S(1)} %copy-done.5), channel_id=2, replica_groups=mesh['tile'=8,'win'=4] {'tile'}, dimensions={0}, use_global_device_ids=true | all-gather | bytes 9216 | tf_op jit(solution)/shard_map/all_gather | solution.py:143
  250.9 16.8 %all-gather.3 = s32[8,1,256]{2,1,0:T(1,128)S(1)} all-gather(s32[1,1,256]{2,1,0:T(1,128)S(1)} %bitcast.111), channel_id=3, replica_groups=mesh['tile'=8,'win'=4] {'tile'}, dimensions={0}, use_global_device_ids=true | all-gather | bytes 9216 | tf_op jit(solution)/shard_map/all_gather | solution.py:141
  267.7 18.0 %all-gather.4 = s32[8,1,256]{2,1,0:T(1,128)S(1)} all-gather(s32[1,1,256]{2,1,0:T(1,128)S(1)} %bitcast.112), channel_id=4, replica_groups=mesh['tile'=8,'win'=4] {'tile'}, dimensions={0}, use_global_device_ids=true | all-gather | bytes 9216 | tf_op jit(solution)/shard_map/all_gather | solution.py:142
  286.0 5.1 %fusion.11 = f32[4,2048,256]{2,1,0:T(8,128)S(1)} fusion(bf16[4,2048,128]{1,2,0:T(8,128)(2,1)} %collective-permute-done.1, bf16[4,2048,256]{1,2,0:T(8,128)(2,1)} %copy-done.1, bf16[4,2048,128]{1,2,0:T(8,128)(2,1)} %collective-permute-done, s32[256]{0:T(256)S(1)} %bitcast.114), kind=kOutput, calls=%fused_computation.23 | convolution fusion | flops 2172780544 | bytes 16778240 | tf_op jit(solution)/shard_map/sfc,cp->sfp/dot_general | solution.py:150
  291.2 6.2 %fusion.10 = f32[4,2048,256]{2,1,0:T(8,128)} fusion(bf16[4,2048,128]{1,2,0:T(8,128)(2,1)} %collective-permute-done.1, bf16[4,2048,256]{1,2,0:T(8,128)(2,1)S(1)} %copy-done.2, bf16[4,2048,128]{1,2,0:T(8,128)(2,1)} %collective-permute-done, s32[256]{0:T(256)S(1)} %bitcast.113), kind=kOutput, calls=%fused_computation.22 | convolution fusion | flops 2172780544 | bytes 16778240 | tf_op jit(solution)/shard_map/sfc,cp->sfp/dot_general | solution.py:153
  297.4 4.0 %multiply_add_fusion = (f32[4,1024,256]{2,1,0:T(8,128)S(1)}, f32[4,1024,256]{2,1,0:T(8,128)S(1)}) fusion(f32[4,2048,256]{2,1,0:T(8,128)} %fusion.10, f32[4,2048,256]{2,1,0:T(8,128)S(1)} %fusion.11), kind=kLoop, calls=%fused_computation.21 | loop fusion | flops 6291456 | bytes 25165824 | tf_op jit(solution)/shard_map/add | solution.py:61
  301.4 2.0 maximum_reduce_fusion
  304.6 1.6 bitcast_multiply_fusion
  306.2 46.0 %all-reduce.2.cloned.1.call-done = f32[2048,256]{1,0:T(8,128)} async-done(((f32[2048,256]{1,0:T(8,128)}), f32[2048,256]{1,0:T(8,128)}) %all-reduce.2.cloned.1.call-update) | async-done | bytes 2097168 | tf_op jit(solution)/shard_map/psum | solution.py:158
  352.2 8.9 %fusion.12 = bf16[512,256]{1,0:T(8,128)(2,1)S(1)} fusion(f32[2048,256]{1,0:T(8,128)} %all-reduce.2.cloned.1.call-done, f32[512,1024]{0,1:T(8,128)S(1)} %get-tuple-element.23, f32[512,1024]{0,1:T(8,128)} %get-tuple-element.24), kind=kOutput, calls=%fused_computation.29 | convolution fusion | flops 3222405120 | bytes 6553600 | tf_op jit(solution)/shard_map/dot_general | solution.py:160
  361.5 22.8 %all_to_all.23 = bf16[8,80,512]{2,1,0:T(8,128)(2,1)S(1)} all-to-all(bf16[8,80,512]{2,1,0:T(8,128)(2,1)S(1)} %bitcast.106), channel_id=1, replica_groups=mesh['tile'=8,'win'=4] {'tile'}, dimensions={0} | all-to-all | bytes 1310720 | tf_op jit(solution)/shard_map/all_to_all | solution.py:170
  (65 shorter events, 9.7 us)
Async XLA Ops:
  10.8 6.3 %slice-start = ((bf16[4,256,2048]{2,1,0:T(8,128)(2,1)}), bf16[4,256,128]{2,1,0:T(8,128)(2,1)S(1)}, s32[]{:S(2)}) async-start(bf16[4,256,2048]{2,1,0:T(8,128)(2,1)} %param.5), calls=%async_computation.3 | async-start | bytes 524288 | tf_op jit(solution)/shard_map/jit(_roll_static)/slice | solution.py:126
  37.2 100.6 %all-to-all-start = ((bf16[4,256,2048]{1,0,2:T(4,128)(2,1)}), bf16[4,256,2048]{1,0,2:T(4,128)(2,1)}, u32[]{:S(2)}, u32[]{:S(2)}) async-start(bf16[4,256,2048]{1,0,2:T(4,128)(2,1)} %copy.52), calls=%async_computation | async-start | bytes 8388608 | tf_op jit(solution)/shard_map/all_to_all | solution.py:134
  44.5 307.7 %all-reduce.2.cloned.1.call-start = ((), (), s32[]{:S(2)}) async-start(), calls=%async_computation.2 | async-start | bytes 4194304 | tf_op jit(solution)/shard_map/psum | solution.py:158
  140.5 3.7 copy-start.3
  156.0 3.2 copy-start
  184.9 2.6 copy-start.1
  184.9 4.7 %copy-start.8 = (s32[8]{0:T(128)S(1)}, s32[8]{0:T(128)}, u32[]{:S(2)}) copy-start(s32[8]{0:T(128)} %constant.94.clone) | copy-start | bytes 100
  184.9 6.5 %copy-start.5 = (s32[256,1]{0,1:T(1,128)S(1)}, s32[256,1]{0,1:T(1,128)}, u32[]{:S(2)}) copy-start(s32[256,1]{0,1:T(1,128)} %param.8) | copy-start | bytes 3076
  184.9 66.0 %copy-start.6 = (s32[256]{0:T(256)S(1)}, s32[256]{0:T(256)}, u32[]{:S(2)}) copy-start(s32[256]{0:T(256)} %param.6) | copy-start | bytes 3076
  184.9 82.8 %copy-start.7 = (s32[256]{0:T(256)S(1)}, s32[256]{0:T(256)}, u32[]{:S(2)}) copy-start(s32[256]{0:T(256)} %param.7) | copy-start | bytes 3076
  187.5 98.5 %collective-permute-start = (bf16[4,2048,128]{1,2,0:T(8,128)(2,1)}, bf16[4,2048,128]{1,2,0:T(8,128)(2,1)}, u32[]{:S(2)}, u32[]{:S(2)}) collective-permute-start(bf16[4,2048,128]{1,2,0:T(8,128)(2,1)} %get-tuple-element.7), channel_id=1, source_target_pairs={{0,4},{4,12},{12,20},{20,28},{28,24},{24,16},{16,8},{8,0},{1,5},{5... | collective-permute-start | bytes 6291464 | tf_op jit(solution)/shard_map/ppermute | solution.py:138
  189.0 97.1 %collective-permute-start.1 = (bf16[4,2048,128]{1,2,0:T(8,128)(2,1)S(1)}, bf16[4,2048,128]{1,2,0:T(8,128)(2,1)}, u32[]{:S(2)}, u32[]{:S(2)}) collective-permute-start(bf16[4,2048,128]{1,2,0:T(8,128)(2,1)S(1)} %get-tuple-element.8), channel_id=1, source_target_pairs={{0,8},{4,0},{12,4},{20,12},{28,20},{24,28},{16,24},{8,16},{1,9},{5... | collective-permute-start | bytes 6291464 | tf_op jit(solution)/shard_map/ppermute | solution.py:139
  286.0 5.1 %copy-start.2 = (bf16[4,2048,256]{1,2,0:T(8,128)(2,1)S(1)}, bf16[4,2048,256]{1,2,0:T(8,128)(2,1)}, u32[]{:S(2)}) copy-start(bf16[4,2048,256]{1,2,0:T(8,128)(2,1)} %copy-done.1) | copy-start | bytes 12582916
  384.4 0.8 copy-start.4
Sparse Core Ops, SparseCore 0:
  303.6 48.6 all-reduce.1
where the time goes:
time: 393 us; the launch traced here: 392 us
  waiting for transfers between devices  119 us (30%)
  blocking collectives  114 us (29%)
  local copies, waits for them, and re-layouts  68.7 us (17%)
  other arithmetic  32.3 us (8%)
  matrix products  32.3 us (8%)
  between operations  15.7 us (4%)
  starting transfers between devices  9.37 us (2%)
    all_to_all x1, waiting for transfers between devices, per_device(): lax.all_to_all(outgoing, 'tile', split_axis=2, concat_axis=1, tiled=True)  73.5 us
    all_gather x1, blocking collectives, per_device(): all_owners = lax.all_gather(owners[:, 0], 'tile')  56.6 us
    psum x1, waiting for transfers between devices, per_device(): stacked = lax.psum(cross, 'win')  46 us
    all_to_all x1, blocking collectives, per_device(): lax.all_to_all(buckets, 'tile', split_axis=0, concat_axis=0, tiled=True)  22.8 us
    all_gather x1, blocking collectives, per_device(): all_offset = lax.all_gather(pair_offset, 'tile')  18 us
    concatenate x2, local copies, waits for them, and re-layouts, per_device(): outgoing = jnp.concatenate([shifted[:, :, b] for b in block_of], axis=2)  17.2 us
    all_gather x1, blocking collectives, per_device(): all_first = lax.all_gather(pair_first, 'tile')  16.8 us
    unnamed x33, local copies, waits for them, and re-layouts  12.3 us
  transfers between devices with their start and end apart: 4, of which 2 were waited for; matrix products, arithmetic and copies ran while one was open for 7% of the time, Pallas kernels for 0%

commit v1 on v0

--- a/solution.py
+++ b/solution.py
@@ -155,7 +155,10 @@
         )
         cross = jnp.sum(cross_terms(first_part, second_part), axis=0)
         lag_count = length // win_count
-        stacked = lax.psum(cross, "win")
+        devices, stacked = (lax.axis_size("win"), cross)
+        for hop in [1 << k_2 for k_2 in range(devices.bit_length() - 1)]:
+            swap = [(i_2, i_2 ^ hop) for i_2 in range(devices)]
+            stacked = stacked + lax.ppermute(stacked, "win", swap)
         inverse = inverse_matrix(length, lax.axis_index("win") * lag_count, lag_count, seg_total)
         correlation = jnp.dot(inverse, stacked, precision=lax.Precision.HIGHEST)
         capacity = 5 * pair_first.shape[0] // (2 * tile_count)

time: 393 us -> 369 us (0.939)
  between operations: 15.7 us -> 2.35 us
  blocking collectives: 114 us -> 107 us
  waiting for transfers between devices: 119 us -> 115 us
    psum x1 -> x0, waiting for transfers between devices: 46 us -> none  [per_device(): stacked = lax.psum(cross, 'win')]
    ppermute x0 -> x2, waiting for transfers between devices: none -> 40.9 us  [per_device(): stacked = stacked + lax.ppermute(stacked, 'win', swap)]
    all_gather x1, blocking collectives: 16.8 us -> 55.9 us  [per_device(): all_first = lax.all_gather(pair_first, 'tile')]
    all_gather x1, blocking collectives: 56.6 us -> 17.8 us  [per_device(): all_owners = lax.all_gather(owners[:, 0], 'tile')]
    all_to_all x1, blocking collectives: 22.8 us -> 16.5 us  [per_device(): lax.all_to_all(buckets, 'tile', split_axis=0, concat_axis=0, tiled=True)]
  transfers between devices with their start and end apart: 4 -> 5, of which waited for: 2 -> 2; matrix products, arithmetic and copies ran while one was open for 7% -> 7% of each run, Pallas kernels for 0% -> 0%
where the time goes in v1:
time: 369 us; the launch traced here: 368 us
  waiting for transfers between devices  115 us (31%)
  blocking collectives  107 us (29%)
  local copies, waits for them, and re-layouts  68.7 us (19%)
  other arithmetic  32.7 us (9%)
  matrix products  31.8 us (9%)
  starting transfers between devices  10.9 us (3%)
    all_to_all x1, waiting for transfers between devices, per_device(): lax.all_to_all(outgoing, 'tile', split_axis=2, concat_axis=1, tiled=True)  73.7 us
    all_gather x1, blocking collectives, per_device(): all_first = lax.all_gather(pair_first, 'tile')  55.9 us
    ppermute x2, waiting for transfers between devices, per_device(): stacked = stacked + lax.ppermute(stacked, 'win', swap)  40.9 us
    all_gather x1, blocking collectives, per_device(): all_owners = lax.all_gather(owners[:, 0], 'tile')  17.8 us
    concatenate x2, local copies, waits for them, and re-layouts, per_device(): outgoing = jnp.concatenate([shifted[:, :, b] for b in block_of], axis=2)  17.2 us
    all_gather x1, blocking collectives, per_device(): all_offset = lax.all_gather(pair_offset, 'tile')  16.8 us
    all_to_all x1, blocking collectives, per_device(): lax.all_to_all(buckets, 'tile', split_axis=0, concat_axis=0, tiled=True)  16.5 us
    unnamed x33, local copies, waits for them, and re-layouts  12.3 us
  transfers between devices with their start and end apart: 5, of which 2 were waited for; matrix products, arithmetic and copies ran while one was open for 7% of the time, Pallas kernels for 0%

profile of v1, /device:TPU:0, one launch (start us, length us, event | category | flops | bytes accessed | tf_op | source)
XLA Modules:
  0.0 368.0 jit_solution(16272401458797594602)
XLA Ops:
  0.0 4.3 %slice.87 = bf16[4,256,1920]{2,1,0:T(8,128)(2,1)} slice(bf16[4,256,2048]{2,1,0:T(8,128)(2,1)} %param.5), slice={[0:4], [0:256], [128:2048]} | slice | bytes 7864320 | tf_op jit(solution)/shard_map/jit(_roll_static)/slice | solution.py:126
  4.3 6.3 %copy.65 = bf16[4,256,1920]{1,2,0:T(8,128)(2,1)} copy(bf16[4,256,1920]{2,1,0:T(8,128)(2,1)} %slice.87) | data formatting | bytes 7864320
  10.8 2.4 pad_maximum_fusion.1
  13.5 17.2 %copy.52 = bf16[4,256,2048]{1,0,2:T(4,128)(2,1)} copy(bf16[4,256,2048]{1,2,0:T(8,128)(2,1)S(1)} %fusion.18) | data formatting | bytes 8388608 | tf_op jit(solution)/shard_map/concatenate | solution.py:129
  30.7 7.3 %all-to-all-start = ((bf16[4,256,2048]{1,0,2:T(4,128)(2,1)}), bf16[4,256,2048]{1,0,2:T(4,128)(2,1)}, u32[]{:S(2)}, u32[]{:S(2)}) async-start(bf16[4,256,2048]{1,0,2:T(4,128)(2,1)} %copy.52), calls=%async_computation | async-start | bytes 8388608 | tf_op jit(solution)/shard_map/all_to_all | solution.py:134
  39.6 5.0 %subtract_convert_fusion = (bf16[1024,32,64]{0,2,1:T(8,128)(2,1)}, bf16[1024,32,64]{0,2,1:T(8,128)(2,1)}) fusion(f32[1024,64]{0,1:T(8,128)S(1)} %get-tuple-element.21, f32[1024,32]{0,1:T(8,128)S(1)} %get-tuple-element.20, f32[1024,64]{0,1:T(8,128)S(1)} %get-tuple-element.22, f32[1024,32]{0,1:T(8,128)S(1)} %get-tuple-element.19), kind=kLoop, calls=%fused_computation.9 | loop fusion | flops 18874368 | bytes 9175040 | tf_op jit(solution)/shard_map/convert.3
  44.6 6.5 %copy.55 = bf16[1024,2048]{1,0:T(8,128)(2,1)} copy(bf16[1024,2048]{0,1:T(8,128)(2,1)} %bitcast.101) | data formatting | bytes 8388608 | tf_op jit(solution)/shard_map/sub | solution.py:21
  51.1 6.5 %copy.56 = bf16[1024,2048]{1,0:T(8,128)(2,1)} copy(bf16[1024,2048]{0,1:T(8,128)(2,1)} %bitcast.100) | data formatting | bytes 8388608 | tf_op jit(solution)/shard_map/neg | solution.py:28
  57.6 73.7 %all-to-all-done = bf16[4,256,2048]{1,0,2:T(4,128)(2,1)} async-done(((bf16[4,256,2048]{1,0,2:T(4,128)(2,1)}), bf16[4,256,2048]{1,0,2:T(4,128)(2,1)}, u32[]{:S(2)}, u32[]{:S(2)}) %all-to-all-start) | async-done | bytes 4194336 | tf_op jit(solution)/shard_map/all_to_all | solution.py:134
  131.3 2.7 copy.53
  134.0 2.7 copy.73
  137.7 11.8 %fusion.4 = f32[4,2048,256]{1,2,0:T(8,128)S(1)} fusion(bf16[4,2048,256]{1,2,0:T(8,128)(2,1)} %bitcast.104, bf16[1024,2048]{1,0:T(8,128)(2,1)} %copy.56, bf16[1024,2048]{1,0:T(8,128)(2,1)S(1)} %copy-done.3), kind=kOutput, calls=%fused_computation.10 | convolution fusion | flops 8606711808 | bytes 20971520 | tf_op jit(solution)/shard_map/fn,snc->sfc/dot_general | solution.py:131
  149.5 3.2 copy-done
  152.7 2.9 fusion.5
  155.6 5.4 %copy.57 = f32[4,1024,256]{2,1,0:T(8,128)} copy(f32[4,1024,256]{1,2,0:T(8,128)} %fusion.5) | data formatting | bytes 8388608 | tf_op jit(solution)/shard_map/add | solution.py:46
  161.0 2.7 bitcast_reduce_fusion
  163.8 2.3 broadcast_in_dim.12
  166.1 5.4 %copy.58 = f32[4,1024,256]{1,2,0:T(8,128)} copy(f32[4,1024,256]{2,1,0:T(8,128)} %bitcast.103) | data formatting | bytes 8388608 | tf_op jit(solution)/shard_map/reshape | solution.py:49
  171.5 7.0 %fusion.3 = bf16[4,2048,256]{1,2,0:T(8,128)(2,1)S(1)} fusion(f32[4,2048,256]{1,2,0:T(8,128)} %copy-done, f32[4,1024,256]{1,2,0:T(8,128)} %copy.58), kind=kLoop, calls=%fused_computation.5 | loop fusion | flops 6291456 | bytes 16777216 | tf_op jit(solution)/shard_map/convert_element_type | solution.py:52
  178.6 2.1 fusion.69
  181.1 1.5 collective-permute-start
  185.7 55.9 %all-gather.3 = s32[8,1,256]{2,1,0:T(1,128)S(1)} all-gather(s32[1,1,256]{2,1,0:T(1,128)S(1)} %bitcast.110), channel_id=3, replica_groups=mesh['tile'=8,'win'=4] {'tile'}, dimensions={0}, use_global_device_ids=true | all-gather | bytes 9216 | tf_op jit(solution)/shard_map/all_gather | solution.py:141
  241.7 16.8 %all-gather.4 = s32[8,1,256]{2,1,0:T(1,128)S(1)} all-gather(s32[1,1,256]{2,1,0:T(1,128)S(1)} %bitcast.111), channel_id=4, replica_groups=mesh['tile'=8,'win'=4] {'tile'}, dimensions={0}, use_global_device_ids=true | all-gather | bytes 9216 | tf_op jit(solution)/shard_map/all_gather | solution.py:142
  258.5 5.1 %fusion.11 = f32[4,2048,256]{2,1,0:T(8,128)S(1)} fusion(bf16[4,2048,128]{1,2,0:T(8,128)(2,1)} %collective-permute-done.1, bf16[4,2048,256]{1,2,0:T(8,128)(2,1)} %copy-done.1, bf16[4,2048,128]{1,2,0:T(8,128)(2,1)} %collective-permute-done, s32[256]{0:T(256)S(1)} %bitcast.113), kind=kOutput, calls=%fused_computation.23 | convolution fusion | flops 2172780544 | bytes 16778240 | tf_op jit(solution)/shard_map/sfc,cp->sfp/dot_general | solution.py:150
  263.6 6.3 %fusion.10 = f32[4,2048,256]{2,1,0:T(8,128)} fusion(bf16[4,2048,128]{1,2,0:T(8,128)(2,1)} %collective-permute-done.1, bf16[4,2048,256]{1,2,0:T(8,128)(2,1)S(1)} %copy-done.2, bf16[4,2048,128]{1,2,0:T(8,128)(2,1)} %collective-permute-done, s32[256]{0:T(256)S(1)} %bitcast.112), kind=kOutput, calls=%fused_computation.22 | convolution fusion | flops 2172780544 | bytes 16778240 | tf_op jit(solution)/shard_map/sfc,cp->sfp/dot_general | solution.py:153
  269.9 4.0 %multiply_add_fusion = (f32[4,1024,256]{2,1,0:T(8,128)S(1)}, f32[4,1024,256]{2,1,0:T(8,128)S(1)}) fusion(f32[4,2048,256]{2,1,0:T(8,128)} %fusion.10, f32[4,2048,256]{2,1,0:T(8,128)S(1)} %fusion.11), kind=kLoop, calls=%fused_computation.21 | loop fusion | flops 6291456 | bytes 25165824 | tf_op jit(solution)/shard_map/add | solution.py:61
  274.7 17.8 %all-gather = s32[2048,1]{0,1:T(1,128)S(1)} all-gather(s32[256,1]{0,1:T(1,128)S(1)} %copy-done.7), channel_id=2, replica_groups=mesh['tile'=8,'win'=4] {'tile'}, dimensions={0}, use_global_device_ids=true | all-gather | bytes 9216 | tf_op jit(solution)/shard_map/all_gather | solution.py:143
  294.3 3.2 add.138
  297.4 1.5 collective-permute-start.3
  301.0 40.9 %collective-permute-done.3 = f32[2048,256]{1,0:T(8,128)S(1)} collective-permute-done((f32[2048,256]{1,0:T(8,128)}, f32[2048,256]{1,0:T(8,128)S(1)}, u32[]{:S(2)}, u32[]{:S(2)}) %collective-permute-start.3) | collective-permute-done | bytes 2097184 | tf_op jit(solution)/shard_map/ppermute | solution.py:161
  341.9 8.3 %fusion.13 = bf16[512,256]{1,0:T(8,128)(2,1)S(1)} fusion(f32[2048,256]{1,0:T(8,128)} %add.138, f32[2048,256]{1,0:T(8,128)S(1)} %collective-permute-done.3, f32[512,1024]{0,1:T(8,128)S(1)} %get-tuple-element.23, f32[512,1024]{0,1:T(8,128)S(1)} %get-tuple-element.24), kind=kOutput, calls=%fused_computation.30 | convolution fusion | flops 3222929408 | bytes 8650752 | tf_op jit(solution)/shard_map/dot_general | solution.py:163
  350.6 16.5 %all_to_all.23 = bf16[8,80,512]{2,1,0:T(8,128)(2,1)S(1)} all-to-all(bf16[8,80,512]{2,1,0:T(8,128)(2,1)S(1)} %bitcast.105), channel_id=1, replica_groups=mesh['tile'=8,'win'=4] {'tile'}, dimensions={0} | all-to-all | bytes 1310720 | tf_op jit(solution)/shard_map/all_to_all | solution.py:173
  (67 shorter events, 10.6 us)
Async XLA Ops:
  4.3 6.3 %slice-start = ((bf16[4,256,2048]{2,1,0:T(8,128)(2,1)}), bf16[4,256,128]{2,1,0:T(8,128)(2,1)S(1)}, s32[]{:S(2)}) async-start(bf16[4,256,2048]{2,1,0:T(8,128)(2,1)} %param.5), calls=%async_computation.2 | async-start | bytes 524288 | tf_op jit(solution)/shard_map/jit(_roll_static)/slice | solution.py:126
  30.7 100.6 %all-to-all-start = ((bf16[4,256,2048]{1,0,2:T(4,128)(2,1)}), bf16[4,256,2048]{1,0,2:T(4,128)(2,1)}, u32[]{:S(2)}, u32[]{:S(2)}) async-start(bf16[4,256,2048]{1,0,2:T(4,128)(2,1)} %copy.52), calls=%async_computation | async-start | bytes 8388608 | tf_op jit(solution)/shard_map/all_to_all | solution.py:134
  134.0 3.7 %copy-start.3 = (bf16[1024,2048]{1,0:T(8,128)(2,1)S(1)}, bf16[1024,2048]{1,0:T(8,128)(2,1)}, u32[]{:S(2)}) copy-start(bf16[1024,2048]{1,0:T(8,128)(2,1)} %copy.55) | copy-start | bytes 12582916
  149.5 3.2 copy-start
  178.5 2.6 copy-start.1
  178.5 4.7 %copy-start.8 = (s32[8]{0:T(128)S(1)}, s32[8]{0:T(128)}, u32[]{:S(2)}) copy-start(s32[8]{0:T(128)} %constant.94.clone) | copy-start | bytes 100
  178.5 7.2 %copy-start.5 = (s32[256]{0:T(256)S(1)}, s32[256]{0:T(256)}, u32[]{:S(2)}) copy-start(s32[256]{0:T(256)} %param.6) | copy-start | bytes 3076
  178.5 63.1 %copy-start.6 = (s32[256]{0:T(256)S(1)}, s32[256]{0:T(256)}, u32[]{:S(2)}) copy-start(s32[256]{0:T(256)} %param.7) | copy-start | bytes 3076
  181.1 77.3 %collective-permute-start = (bf16[4,2048,128]{1,2,0:T(8,128)(2,1)}, bf16[4,2048,128]{1,2,0:T(8,128)(2,1)}, u32[]{:S(2)}, u32[]{:S(2)}) collective-permute-start(bf16[4,2048,128]{1,2,0:T(8,128)(2,1)} %get-tuple-element.7), channel_id=1, source_target_pairs={{0,4},{4,12},{12,20},{20,28},{28,24},{24,16},{16,8},{8,0},{1,5},{5... | collective-permute-start | bytes 6291464 | tf_op jit(solution)/shard_map/ppermute | solution.py:138
  182.6 75.9 %collective-permute-start.1 = (bf16[4,2048,128]{1,2,0:T(8,128)(2,1)S(1)}, bf16[4,2048,128]{1,2,0:T(8,128)(2,1)}, u32[]{:S(2)}, u32[]{:S(2)}) collective-permute-start(bf16[4,2048,128]{1,2,0:T(8,128)(2,1)S(1)} %get-tuple-element.8), channel_id=1, source_target_pairs={{0,8},{4,0},{12,4},{20,12},{28,20},{24,28},{16,24},{8,16},{1,9},{5... | collective-permute-start | bytes 6291464 | tf_op jit(solution)/shard_map/ppermute | solution.py:139
  258.5 5.1 %copy-start.2 = (bf16[4,2048,256]{1,2,0:T(8,128)(2,1)S(1)}, bf16[4,2048,256]{1,2,0:T(8,128)(2,1)}, u32[]{:S(2)}) copy-start(bf16[4,2048,256]{1,2,0:T(8,128)(2,1)} %copy-done.1) | copy-start | bytes 12582916
  273.9 0.8 copy-start.7
  274.6 19.7 %collective-permute-start.2 = (f32[2048,256]{1,0:T(8,128)S(1)}, f32[2048,256]{1,0:T(8,128)}, u32[]{:S(2)}, u32[]{:S(2)}) collective-permute-start(f32[2048,256]{1,0:T(8,128)S(1)} %maximum_reduce_fusion), channel_id=1, source_target_pairs={{0,1},{1,0},{2,3},{3,2},{4,5},{5,4},{6,7},{7,6},{8,9},{9,8},{10,11... | collective-permute-start | bytes 6291464 | tf_op jit(solution)/shard_map/ppermute | solution.py:161
  297.4 44.5 %collective-permute-start.3 = (f32[2048,256]{1,0:T(8,128)}, f32[2048,256]{1,0:T(8,128)S(1)}, u32[]{:S(2)}, u32[]{:S(2)}) collective-permute-start(f32[2048,256]{1,0:T(8,128)} %add.138), channel_id=1, source_target_pairs={{0,2},{1,3},{2,0},{3,1},{4,6},{5,7},{6,4},{7,5},{8,10},{9,11},{10,... | collective-permute-start | bytes 6291464 | tf_op jit(solution)/shard_map/ppermute | solution.py:161
  367.1 0.8 copy-start.4
